TPU v7x, 256 devices: a whole 4x4x8 slice. The times are simulated.
256 devices in a mesh: dp: 64 (over x, z, core), tensor: 4 (over y).
Axes of the slice: x: 4, y: 4, z: 8, core: 2. Of those that a mesh axis runs over, the one named last changes fastest.
Arguments:
- attention_grads: bfloat16 [64, 1, 512, 2048], P('dp', None, None, 'tensor')
- expert_grads: bfloat16 [64, 1, 2, 512, 4096], P('dp', None, None, None, 'tensor')
- routing_grads: bfloat16 [64, 4, 1, 36, 512], P('dp', 'tensor'), may hold values from -640 to 640
- attention_master: float32 [512, 2048], P('dp', 'tensor'), may hold values from -0.25 to 0.25
- attention_first: float32 [512, 2048], P('dp', 'tensor'), may hold values from -4 to 4
- attention_second: float32 [512, 2048], P('dp', 'tensor'), may hold values from 0.05 to 2
- expert_master: float32 [2, 512, 4096], P(None, 'dp', 'tensor'), may hold values from -0.25 to 0.25
- expert_first: float32 [2, 512, 4096], P(None, 'dp', 'tensor'), may hold values from -4 to 4
- expert_second: float32 [2, 512, 4096], P(None, 'dp', 'tensor'), may hold values from 0.05 to 2
- routing_master: float32 [36, 512], P(None, ('dp', 'tensor')), may hold values from -4 to 4
- routing_first: float32 [36, 512], P(None, ('dp', 'tensor')), may hold values from -4 to 4
- routing_second: float32 [36, 512], P(None, ('dp', 'tensor')), may hold values from 0.05 to 2
- step_count: int32 [1], replicated, may hold values from 1 to 1000
- learn_rate: float32 [1], replicated, may hold values from 0.05 to 0.3
- clip_level: float32 [1], replicated, may hold values from 0.5 to 2
Outputs:
- attention_renewed: float32 [512, 2048], P('dp', 'tensor')
- attention_momentum: float32 [512, 2048], P('dp', 'tensor')
- attention_variance: float32 [512, 2048], P('dp', 'tensor')
- attention_served: bfloat16 [512, 2048], P(None, 'tensor')
- expert_renewed: float32 [2, 512, 4096], P(None, 'dp', 'tensor')
- expert_momentum: float32 [2, 512, 4096], P(None, 'dp', 'tensor')
- expert_variance: float32 [2, 512, 4096], P(None, 'dp', 'tensor')
- expert_served: bfloat16 [2, 512, 4096], P(None, None, 'tensor')
- routing_renewed: float32 [36, 512], P(None, ('dp', 'tensor'))
- routing_momentum: float32 [36, 512], P(None, ('dp', 'tensor'))
- routing_variance: float32 [36, 512], P(None, ('dp', 'tensor'))
- routing_served: bfloat16 [36, 512], replicated
Inputs may be any that keep to these rules, and one draw needn't show every extreme that they name: `step_count`: the number of optimizer steps taken, this one included.
All inputs are finite; a program needn't handle non-finite values.
Results may differ from a plain program's by a relative error of at most 0.0004.
Values may be sent and summed in bfloat16 or wider, within the bound.
No kernel may reach another device: no remote copies, remote signals or barrier semaphores. Data moves between devices by JAX's collectives and lax.ppermute only.
A program may use at most 64 MiB of HBM per device.

v0:
```python
import jax
import jax.numpy as jnp
from jax import lax
from jax.sharding import Mesh, PartitionSpec as P

EXPERTS = 32
PARAMS = 5261312
BETA_ONE = 0.9
BETA_TWO = 0.999
EPSILON = 1e-08
DECAY = 0.1
DP_PARTS = ("dp_x", "dp_z", "dp_core")
DP = DP_PARTS


def adam_update(grad_sum, master, first, second, clip, rate, first_fix, second_fix, mask):
    grad = clip * grad_sum
    momentum = BETA_ONE * first + (1.0 - BETA_ONE) * grad
    variance = BETA_TWO * second + (1.0 - BETA_TWO) * grad * grad
    update = (
        momentum / first_fix / (jnp.sqrt(variance / second_fix) + EPSILON) + DECAY * mask * master
    )
    renewed = master - rate * update
    return (renewed, momentum, variance, renewed.astype(jnp.bfloat16))


def local(
    attention_grads,
    expert_grads,
    routing_grads,
    attention_master,
    attention_first,
    attention_second,
    expert_master,
    expert_first,
    expert_second,
    routing_master,
    routing_first,
    routing_second,
    step_count,
    learn_rate,
    clip_level,
):
    n_dp = lax.axis_size(DP)
    n_t = lax.axis_size("tensor")
    t_idx = lax.axis_index("tensor")
    att = attention_grads[0, 0]
    exp = expert_grads[0, 0]
    rte = routing_grads[0, 0, 0]
    rows, cols = att.shape
    n_e, e_rows, e_cols = exp.shape
    n_r, r_cols = rte.shape
    ra = rows // n_dp
    re = e_rows // n_dp
    rc = r_cols // n_dp
    own = rc // n_t
    exp_rows = exp.transpose(1, 0, 2).reshape(e_rows, n_e * e_cols)
    send = jnp.concatenate([att, exp_rows, rte.T], axis=1)
    got = lax.all_to_all(send, DP, 0, 0, tiled=True)
    total = jnp.sum(got.reshape(n_dp, ra, -1).astype(jnp.float32), axis=0)
    attention_sum = total[:, :cols]
    expert_sum = total[:, cols : cols + n_e * e_cols].reshape(re, n_e, e_cols).transpose(1, 0, 2)
    route_part = total[:, cols + n_e * e_cols :].T
    local_squares = jnp.sum(attention_sum * attention_sum) + jnp.sum(expert_sum * expert_sum)
    slot = (jnp.arange(rc) // own == t_idx)[None, :]

    def placed(values):
        return jnp.where(slot, jnp.tile(values, (1, n_t)), 0.0)

    packed = jnp.stack(
        [
            route_part,
            placed(routing_master),
            placed(routing_first),
            placed(routing_second),
            jnp.full((n_r, rc), 0.0).at[0, 0].set(local_squares),
        ]
    )
    packed = lax.psum(packed, "tensor")
    route_sum = packed[0]
    route_master_blk, route_first_blk, route_second_blk = (packed[1], packed[2], packed[3])
    group_squares = packed[4, 0, 0] + jnp.sum(route_sum * route_sum)
    spread = jnp.broadcast_to(group_squares, (n_dp, 1))
    squares = jnp.sum(lax.all_to_all(spread, DP, 0, 0, tiled=True))
    grad_norm = jnp.sqrt(squares)
    clip = jnp.minimum(1.0, clip_level[0] * jnp.sqrt(jnp.float32(PARAMS)) / (grad_norm + 1e-06))
    steps_done = step_count[0].astype(jnp.float32)
    first_fix = 1.0 - jnp.power(jnp.float32(BETA_ONE), steps_done)
    second_fix = 1.0 - jnp.power(jnp.float32(BETA_TWO), steps_done)
    rate = learn_rate[0]
    one = jnp.float32(1.0)
    attention_out = adam_update(
        attention_sum,
        attention_master,
        attention_first,
        attention_second,
        clip,
        rate,
        first_fix,
        second_fix,
        one,
    )
    expert_out = adam_update(
        expert_sum,
        expert_master,
        expert_first,
        expert_second,
        clip,
        rate,
        first_fix,
        second_fix,
        one,
    )
    row_index = jnp.arange(n_r, dtype=jnp.int32)
    routing_mask = (row_index < EXPERTS).astype(jnp.float32)[:, None]
    routing_out = adam_update(
        route_sum,
        route_master_blk,
        route_first_blk,
        route_second_blk,
        clip,
        rate,
        first_fix,
        second_fix,
        routing_mask,
    )

    def mine(values):
        return lax.dynamic_slice_in_dim(values, t_idx * own, own, axis=1)

    def gather(values):
        for name in (DP_PARTS[2], DP_PARTS[1]):
            values = lax.all_gather(values, name, axis=0, tiled=True)
        name = DP_PARTS[0]
        size = lax.axis_size(name)
        ring = [values] + [
            lax.ppermute(values, name, [(i, (i + size - k) % size) for i in range(size)])
            for k in range(1, size)
        ]
        stacked = jnp.stack(ring)
        stacked = jnp.roll(stacked, lax.axis_index(name), axis=0)
        return stacked.reshape((-1,) + values.shape[1:])

    rest = jnp.concatenate(
        [
            attention_out[3],
            expert_out[3].transpose(1, 0, 2).reshape(re, n_e * e_cols),
            routing_out[3].T,
        ],
        axis=1,
    )
    rest = gather(rest)
    attention_served = rest[:, :cols]
    expert_served = (
        rest[:, cols : cols + n_e * e_cols].reshape(e_rows, n_e, e_cols).transpose(1, 0, 2)
    )
    routing_served = rest[:, cols + n_e * e_cols :].T
    return (
        attention_out[0],
        attention_out[1],
        attention_out[2],
        attention_served,
        expert_out[0],
        expert_out[1],
        expert_out[2],
        expert_served,
        mine(routing_out[0]),
        mine(routing_out[1]),
        mine(routing_out[2]),
        routing_served,
    )


def split_mesh(mesh):
    column = mesh.devices[:, 0]
    sizes = (
        len({d.coords[0] for d in column}),
        len({d.coords[2] for d in column}),
        len({d.core_on_chip for d in column}),
    )
    devices = mesh.devices.reshape(sizes + mesh.devices.shape[1:])
    return Mesh(devices, DP_PARTS + ("tensor",))


def solution(mesh):
    mesh = split_mesh(mesh)
    in_specs = (
        P(DP, None, None, "tensor"),
        P(DP, None, None, None, "tensor"),
        P(DP, "tensor", None, None, None),
        P(DP, "tensor"),
        P(DP, "tensor"),
        P(DP, "tensor"),
        P(None, DP, "tensor"),
        P(None, DP, "tensor"),
        P(None, DP, "tensor"),
        P(None, DP + ("tensor",)),
        P(None, DP + ("tensor",)),
        P(None, DP + ("tensor",)),
        P(),
        P(),
        P(),
    )
    out_specs = (
        P(DP, "tensor"),
        P(DP, "tensor"),
        P(DP, "tensor"),
        P(None, "tensor"),
        P(None, DP, "tensor"),
        P(None, DP, "tensor"),
        P(None, DP, "tensor"),
        P(None, None, "tensor"),
        P(None, DP + ("tensor",)),
        P(None, DP + ("tensor",)),
        P(None, DP + ("tensor",)),
        P(),
    )
    return jax.shard_map(local, mesh=mesh, in_specs=in_specs, out_specs=out_specs, check_vma=False)
```

profile of v0, /device:TPU:7, one launch (start us, length us, event | category | flops | bytes accessed | tf_op | source)
XLA Modules:
  0.0 199.6 jit_solution(18282332297180285942)
XLA Ops:
  0.7 1.0 copy.75
  1.6 5.1 %copy.74 = bf16[512,2,1024]{2,1,0:T(2,128)(2,1)} copy(bf16[512,2,1024]{2,0,1:T(8,128)(2,1)} %bitcast.80) | data formatting | bytes 4194304 | tf_op jit(solution)/shard_map/transpose | solution.py:57
  6.7 3.3 %concatenate.21 = bf16[64,8,2048]{2,1,0:T(8,128)(2,1)S(1)} reshape(bf16[512,2,1024]{2,1,0:T(2,128)(2,1)} %copy.74) | data formatting | bytes 4194304 | tf_op jit(solution)/shard_map/concatenate | solution.py:58
  10.0 1.8 pad_maximum_fusion
  11.9 12.6 %all-to-all-start = ((bf16[64,8,2596]{2,1,0:T(8,128)(2,1)}), bf16[64,8,2596]{2,1,0:T(8,128)(2,1)S(1)}, u32[]{:S(2)}, u32[]{:S(2)}) async-start(bf16[64,8,2596]{2,1,0:T(8,128)(2,1)} %pad_maximum_fusion), calls=%async_computation | async-start | bytes 5505024 | tf_op jit(solution)/shard_map/all_to_all | solution.py:59
  26.4 62.9 %all-to-all-done = bf16[64,8,2596]{2,1,0:T(8,128)(2,1)S(1)} async-done(((bf16[64,8,2596]{2,1,0:T(8,128)(2,1)}), bf16[64,8,2596]{2,1,0:T(8,128)(2,1)S(1)}, u32[]{:S(2)}, u32[]{:S(2)}) %all-to-all-start) | async-done | bytes 2658336 | tf_op jit(solution)/shard_map/all_to_all | solution.py:59
  89.9 0.6 multiply_reduce_fusion
  92.7 13.5 %psum.7 = f32[5,36,8]{1,2,0:T(8,128)S(1)} all-reduce(f32[5,36,8]{1,2,0:T(8,128)S(1)} %constant_dynamic-update-slice_fusion), channel_id=1, replica_groups=mesh['dp_x'=4,'dp_z'=8,'dp_core'=2,'tensor'=4] {'tensor'}, use_global_device_ids=true, to_apply=%region_3.4 | all-reduce | flops 1440 | bytes 11520 | tf_op jit(solution)/shard_map/psum | solution.py:79
  108.6 0.6 broadcast_in_dim.28
  109.2 9.5 %all-to-all-start.1 = ((f32[64,1,1]{2,1,0:T(1,128)}), f32[64,1,1]{2,1,0:T(1,128)S(1)}, u32[]{:S(2)}, u32[]{:S(2)}) async-start(f32[64,1,1]{2,1,0:T(1,128)} %broadcast_in_dim.28), calls=%async_computation.1 | async-start | bytes 65536 | tf_op jit(solution)/shard_map/all_to_all | solution.py:84
  118.8 7.2 %all-to-all-done.1 = f32[64,1,1]{2,1,0:T(1,128)S(1)} async-done(((f32[64,1,1]{2,1,0:T(1,128)}), f32[64,1,1]{2,1,0:T(1,128)S(1)}, u32[]{:S(2)}, u32[]{:S(2)}) %all-to-all-start.1) | async-done | bytes 288 | tf_op jit(solution)/shard_map/all_to_all | solution.py:84
  126.0 0.7 reduce_sum.49
  127.4 0.6 fusion.7
  128.1 0.7 fusion.9
  128.8 2.2 %all_gather.6 = bf16[16,2596]{1,0:T(8,128)(2,1)S(1)} all-gather(bf16[8,2596]{1,0:T(8,128)(2,1)S(1)} %pad_maximum_fusion.1), channel_id=1, replica_groups=mesh['dp_x'=4,'dp_z'=8,'dp_core'=2,'tensor'=4] {'dp_core'}, dimensions={0}, use_global_device_ids=true | all-gather | bytes 124608 | tf_op jit(solution)/shard_map/all_gather | solution.py:133
  131.0 20.1 %all_gather.7 = bf16[128,2596]{1,0:T(8,128)(2,1)S(1)} all-gather(bf16[16,2596]{1,0:T(8,128)(2,1)S(1)} %all_gather.6), channel_id=1, replica_groups=mesh['dp_x'=4,'dp_z'=8,'dp_core'=2,'tensor'=4] {'dp_z'}, dimensions={0}, use_global_device_ids=true | all-gather | bytes 747648 | tf_op jit(solution)/shard_map/all_gather | solution.py:133
  151.4 2.0 collective-permute-start.2
  155.5 0.9 bitcast_dynamic-update-slice_fusion.4
  156.4 5.6 %collective-permute-done.2 = bf16[128,2596]{0,1:T(8,128)(2,1)S(1)} collective-permute-done((bf16[128,2596]{0,1:T(8,128)(2,1)S(1)}, bf16[128,2596]{0,1:T(8,128)(2,1)S(1)}, u32[]{:S(2)}, u32[]{:S(2)}) %collective-permute-start.2) | collective-permute-done | bytes 664608 | tf_op jit(solution)/shard_map/ppermute | solution.py:137
  162.4 23.8 %collective-permute-done = bf16[128,2596]{0,1:T(8,128)(2,1)} collective-permute-done((bf16[128,2596]{0,1:T(8,128)(2,1)S(1)}, bf16[128,2596]{0,1:T(8,128)(2,1)}, u32[]{:S(2)}, u32[]{:S(2)}) %collective-permute-start) | collective-permute-done | bytes 664608 | tf_op jit(solution)/shard_map/ppermute | solution.py:137
  186.1 1.4 copy.78
  187.6 0.9 bitcast_dynamic-update-slice_fusion.2
  188.8 0.9 bitcast_dynamic-update-slice_fusion
  189.7 0.9 constant_dynamic-update-slice_fusion.6
  190.6 0.9 bitcast_dynamic-update-slice_fusion.5
  191.5 0.9 bitcast_dynamic-update-slice_fusion.3
  192.5 0.9 bitcast_dynamic-update-slice_fusion.1
  193.4 0.9 constant_dynamic-update-slice_fusion.5
  194.3 2.0 constant_dynamic-slice_fusion.3
  196.3 0.8 slice.68
  197.4 0.7 copy.85
  198.1 1.5 copy.89
  (47 shorter events, 6.0 us)
Async XLA Ops:
  0.6 9.4 %copy-start = (bf16[1,1,512,512]{3,2,1,0:T(8,128)(2,1)S(1)}, bf16[1,1,512,512]{3,2,1,0:T(8,128)(2,1)}, u32[]{:S(2)}) copy-start(bf16[1,1,512,512]{3,2,1,0:T(8,128)(2,1)} %param.17) | copy-start | bytes 1572868
  11.8 80.7 %copy-start.7 = (f32[36,2]{0,1:T(2,128)S(1)}, f32[36,2]{0,1:T(2,128)}, u32[]{:S(2)}) copy-start(f32[36,2]{0,1:T(2,128)} %param.26) | copy-start | bytes 868
  11.8 80.7 %copy-start.8 = (f32[36,2]{0,1:T(2,128)S(1)}, f32[36,2]{0,1:T(2,128)}, u32[]{:S(2)}) copy-start(f32[36,2]{0,1:T(2,128)} %param.27) | copy-start | bytes 868
  11.8 80.8 %copy-start.9 = (f32[36,2]{0,1:T(2,128)S(1)}, f32[36,2]{0,1:T(2,128)}, u32[]{:S(2)}) copy-start(f32[36,2]{0,1:T(2,128)} %param.28) | copy-start | bytes 868
  11.8 115.6 %copy-start.4 = (f32[8,512]{1,0:T(8,128)S(1)}, f32[8,512]{1,0:T(8,128)}, u32[]{:S(2)}) copy-start(f32[8,512]{1,0:T(8,128)} %param.20) | copy-start | bytes 49156
  11.8 115.6 %copy-start.5 = (f32[8,512]{1,0:T(8,128)S(1)}, f32[8,512]{1,0:T(8,128)}, u32[]{:S(2)}) copy-start(f32[8,512]{1,0:T(8,128)} %param.22) | copy-start | bytes 49156
  11.8 115.6 %copy-start.6 = (f32[8,512]{1,0:T(8,128)S(1)}, f32[8,512]{1,0:T(8,128)}, u32[]{:S(2)}) copy-start(f32[8,512]{1,0:T(8,128)} %param.21) | copy-start | bytes 49156
  11.8 116.2 %copy-start.1 = (f32[2,8,1024]{2,1,0:T(8,128)S(1)}, f32[2,8,1024]{2,1,0:T(8,128)}, u32[]{:S(2)}) copy-start(f32[2,8,1024]{2,1,0:T(8,128)} %param.23) | copy-start | bytes 196612
  11.8 116.2 %copy-start.2 = (f32[2,8,1024]{2,1,0:T(8,128)S(1)}, f32[2,8,1024]{2,1,0:T(8,128)}, u32[]{:S(2)}) copy-start(f32[2,8,1024]{2,1,0:T(8,128)} %param.25) | copy-start | bytes 196612
  11.8 116.2 %copy-start.3 = (f32[2,8,1024]{2,1,0:T(8,128)S(1)}, f32[2,8,1024]{2,1,0:T(8,128)}, u32[]{:S(2)}) copy-start(f32[2,8,1024]{2,1,0:T(8,128)} %param.24) | copy-start | bytes 196612
  11.9 77.5 %all-to-all-start = ((bf16[64,8,2596]{2,1,0:T(8,128)(2,1)}), bf16[64,8,2596]{2,1,0:T(8,128)(2,1)S(1)}, u32[]{:S(2)}, u32[]{:S(2)}) async-start(bf16[64,8,2596]{2,1,0:T(8,128)(2,1)} %pad_maximum_fusion), calls=%async_computation | async-start | bytes 5505024 | tf_op jit(solution)/shard_map/all_to_all | solution.py:59
  109.2 16.7 %all-to-all-start.1 = ((f32[64,1,1]{2,1,0:T(1,128)}), f32[64,1,1]{2,1,0:T(1,128)S(1)}, u32[]{:S(2)}, u32[]{:S(2)}) async-start(f32[64,1,1]{2,1,0:T(1,128)} %broadcast_in_dim.28), calls=%async_computation.1 | async-start | bytes 65536 | tf_op jit(solution)/shard_map/all_to_all | solution.py:84
  151.4 10.6 %collective-permute-start.2 = (bf16[128,2596]{0,1:T(8,128)(2,1)S(1)}, bf16[128,2596]{0,1:T(8,128)(2,1)S(1)}, u32[]{:S(2)}, u32[]{:S(2)}) collective-permute-start(bf16[128,2596]{0,1:T(8,128)(2,1)S(1)} %copy.77), channel_id=1, source_target_pairs={{0,64},{64,128},{128,192},{192,0},{1,65},{65,129},{129,193},{193,1... | collective-permute-start | bytes 1993736 | tf_op jit(solution)/shard_map/ppermute | solution.py:137
  153.4 35.1 %collective-permute-start.1 = (bf16[128,2596]{0,1:T(8,128)(2,1)S(1)}, bf16[128,2596]{0,1:T(8,128)(2,1)S(1)}, u32[]{:S(2)}, u32[]{:S(2)}) collective-permute-start(bf16[128,2596]{0,1:T(8,128)(2,1)S(1)} %copy.77), channel_id=1, source_target_pairs={{0,128},{64,192},{128,0},{192,64},{1,129},{65,193},{129,1},{193,65... | collective-permute-start | bytes 1993736 | tf_op jit(solution)/shard_map/ppermute | solution.py:137
  154.0 32.2 %collective-permute-start = (bf16[128,2596]{0,1:T(8,128)(2,1)S(1)}, bf16[128,2596]{0,1:T(8,128)(2,1)}, u32[]{:S(2)}, u32[]{:S(2)}) collective-permute-start(bf16[128,2596]{0,1:T(8,128)(2,1)S(1)} %copy.77), channel_id=1, source_target_pairs={{0,192},{64,0},{128,64},{192,128},{1,193},{65,1},{129,65},{193,129... | collective-permute-start | bytes 1993736 | tf_op jit(solution)/shard_map/ppermute | solution.py:137
where the time goes:
time: 200 us
  waiting for transfers between devices  99.5 us (50%)
  blocking collectives  35.8 us (18%)
  local copies, waits for them, and re-layouts  26.7 us (13%)
  starting transfers between devices  25 us (12%)
  other arithmetic  6.4 us (3%)
  between operations  6.24 us (3%)
    all_to_all x1, waiting for transfers between devices, local(): got = lax.all_to_all(send, DP, 0, 0, tiled=True)  62.9 us
    ppermute x3, waiting for transfers between devices, gather(): lax.ppermute(values, name, [(i, (i + size - k) % size) for i in range(siz...  29.4 us
    all_gather x2, blocking collectives, gather(): values = lax.all_gather(values, name, axis=0, tiled=True)  22.3 us
    psum x1, blocking collectives, local(): packed = lax.psum(packed, 'tensor')  13.5 us
    all_to_all x1, starting transfers between devices, local(): got = lax.all_to_all(send, DP, 0, 0, tiled=True)  12.6 us
    all_to_all x1, starting transfers between devices, local(): squares = jnp.sum(lax.all_to_all(spread, DP, 0, 0, tiled=True))  9.48 us
    all_to_all x1, waiting for transfers between devices, local(): squares = jnp.sum(lax.all_to_all(spread, DP, 0, 0, tiled=True))  7.16 us
    unnamed x29, local copies, waits for them, and re-layouts  7.15 us
  transfers between devices with their start and end apart: 5, of which 4 were waited for; matrix products, arithmetic and copies ran while one was open for 2% of the time, Pallas kernels for 0%

commit v1 on v0

--- a/solution.py
+++ b/solution.py
@@ -76,7 +76,7 @@
             jnp.full((n_r, rc), 0.0).at[0, 0].set(local_squares),
         ]
     )
-    packed = lax.psum(packed, "tensor")
+    packed = jnp.sum(lax.all_gather(packed, "tensor"), axis=0)
     route_sum = packed[0]
     route_master_blk, route_first_blk, route_second_blk = (packed[1], packed[2], packed[3])
     group_squares = packed[4, 0, 0] + jnp.sum(route_sum * route_sum)

time: 200 us -> 195 us (0.975)
  blocking collectives: 35.8 us -> 31.8 us
    psum x1 -> x0, blocking collectives: 13.5 us -> none  [local(): packed = lax.psum(packed, 'tensor')]
    all_gather x0 -> x1, blocking collectives: none -> 9.52 us  [local(): packed = jnp.sum(lax.all_gather(packed, 'tensor'), axis=0)]
where the time goes in v1:
time: 195 us
  waiting for transfers between devices  99.5 us (51%)
  blocking collectives  31.8 us (16%)
  local copies, waits for them, and re-layouts  26.7 us (14%)
  starting transfers between devices  24.2 us (12%)
  other arithmetic  6.42 us (3%)
  between operations  6.24 us (3%)
    all_to_all x1, waiting for transfers between devices, local(): got = lax.all_to_all(send, DP, 0, 0, tiled=True)  62.9 us
    ppermute x3, waiting for transfers between devices, gather(): lax.ppermute(values, name, [(i, (i + size - k) % size) for i in range(siz...  29.4 us
    all_gather x2, blocking collectives, gather(): values = lax.all_gather(values, name, axis=0, tiled=True)  22.3 us
    all_to_all x1, starting transfers between devices, local(): got = lax.all_to_all(send, DP, 0, 0, tiled=True)  12.6 us
    all_gather x1, blocking collectives, local(): packed = jnp.sum(lax.all_gather(packed, 'tensor'), axis=0)  9.52 us
    all_to_all x1, starting transfers between devices, local(): squares = jnp.sum(lax.all_to_all(spread, DP, 0, 0, tiled=True))  8.61 us
    all_to_all x1, waiting for transfers between devices, local(): squares = jnp.sum(lax.all_to_all(spread, DP, 0, 0, tiled=True))  7.16 us
    unnamed x29, local copies, waits for them, and re-layouts  7.15 us
  transfers between devices with their start and end apart: 5, of which 4 were waited for; matrix products, arithmetic and copies ran while one was open for 2% of the time, Pallas kernels for 0%

profile of v1, /device:TPU:7, one launch (start us, length us, event | category | flops | bytes accessed | tf_op | source)
XLA Modules:
  0.0 194.8 jit_solution(13754728327132670927)
XLA Ops:
  0.7 1.0 copy.75
  1.6 5.1 %copy.74 = bf16[512,2,1024]{2,1,0:T(2,128)(2,1)} copy(bf16[512,2,1024]{2,0,1:T(8,128)(2,1)} %bitcast.81) | data formatting | bytes 4194304 | tf_op jit(solution)/shard_map/transpose | solution.py:57
  6.7 3.3 %concatenate.21 = bf16[64,8,2048]{2,1,0:T(8,128)(2,1)S(1)} reshape(bf16[512,2,1024]{2,1,0:T(2,128)(2,1)} %copy.74) | data formatting | bytes 4194304 | tf_op jit(solution)/shard_map/concatenate | solution.py:58
  10.0 1.8 pad_maximum_fusion
  11.9 12.6 %all-to-all-start = ((bf16[64,8,2596]{2,1,0:T(8,128)(2,1)}), bf16[64,8,2596]{2,1,0:T(8,128)(2,1)S(1)}, u32[]{:S(2)}, u32[]{:S(2)}) async-start(bf16[64,8,2596]{2,1,0:T(8,128)(2,1)} %pad_maximum_fusion), calls=%async_computation | async-start | bytes 5505024 | tf_op jit(solution)/shard_map/all_to_all | solution.py:59
  26.4 62.9 %all-to-all-done = bf16[64,8,2596]{2,1,0:T(8,128)(2,1)S(1)} async-done(((bf16[64,8,2596]{2,1,0:T(8,128)(2,1)}), bf16[64,8,2596]{2,1,0:T(8,128)(2,1)S(1)}, u32[]{:S(2)}, u32[]{:S(2)}) %all-to-all-start) | async-done | bytes 2658336 | tf_op jit(solution)/shard_map/all_to_all | solution.py:59
  89.9 0.6 multiply_reduce_fusion
  92.7 9.5 %all-gather = f32[20,36,8]{1,2,0:T(8,128)S(1)} all-gather(f32[5,36,8]{1,2,0:T(8,128)S(1)} %constant_dynamic-update-slice_fusion), channel_id=2, replica_groups=mesh['dp_x'=4,'dp_z'=8,'dp_core'=2,'tensor'=4] {'tensor'}, dimensions={0}, use_global_device_ids=true | all-gather | bytes 28800 | tf_op jit(solution)/shard_map/all_gather | solution.py:79
  104.6 0.6 broadcast_in_dim.28
  105.3 8.6 %all-to-all-start.1 = ((f32[64,1,1]{2,1,0:T(1,128)}), f32[64,1,1]{2,1,0:T(1,128)S(1)}, u32[]{:S(2)}, u32[]{:S(2)}) async-start(f32[64,1,1]{2,1,0:T(1,128)} %broadcast_in_dim.28), calls=%async_computation.1 | async-start | bytes 65536 | tf_op jit(solution)/shard_map/all_to_all | solution.py:84
  114.0 7.2 %all-to-all-done.1 = f32[64,1,1]{2,1,0:T(1,128)S(1)} async-done(((f32[64,1,1]{2,1,0:T(1,128)}), f32[64,1,1]{2,1,0:T(1,128)S(1)}, u32[]{:S(2)}, u32[]{:S(2)}) %all-to-all-start.1) | async-done | bytes 288 | tf_op jit(solution)/shard_map/all_to_all | solution.py:84
  121.1 0.7 reduce_sum.59
  122.6 0.6 fusion.7
  123.3 0.7 fusion.9
  124.0 2.2 %all_gather.14 = bf16[16,2596]{1,0:T(8,128)(2,1)S(1)} all-gather(bf16[8,2596]{1,0:T(8,128)(2,1)S(1)} %pad_maximum_fusion.1), channel_id=1, replica_groups=mesh['dp_x'=4,'dp_z'=8,'dp_core'=2,'tensor'=4] {'dp_core'}, dimensions={0}, use_global_device_ids=true | all-gather | bytes 124608 | tf_op jit(solution)/shard_map/all_gather | solution.py:133
  126.1 20.1 %all_gather.15 = bf16[128,2596]{1,0:T(8,128)(2,1)S(1)} all-gather(bf16[16,2596]{1,0:T(8,128)(2,1)S(1)} %all_gather.14), channel_id=1, replica_groups=mesh['dp_x'=4,'dp_z'=8,'dp_core'=2,'tensor'=4] {'dp_z'}, dimensions={0}, use_global_device_ids=true | all-gather | bytes 747648 | tf_op jit(solution)/shard_map/all_gather | solution.py:133
  146.6 2.0 %collective-permute-start.2 = (bf16[128,2596]{0,1:T(8,128)(2,1)S(1)}, bf16[128,2596]{0,1:T(8,128)(2,1)S(1)}, u32[]{:S(2)}, u32[]{:S(2)}) collective-permute-start(bf16[128,2596]{0,1:T(8,128)(2,1)S(1)} %copy.77), channel_id=1, source_target_pairs={{0,64},{64,128},{128,192},{192,0},{1,65},{65,129},{129,193},{193,1... | collective-permute-start | bytes 1993736 | tf_op jit(solution)/shard_map/ppermute | solution.py:137
  150.7 0.9 bitcast_dynamic-update-slice_fusion.4
  151.6 5.6 %collective-permute-done.2 = bf16[128,2596]{0,1:T(8,128)(2,1)S(1)} collective-permute-done((bf16[128,2596]{0,1:T(8,128)(2,1)S(1)}, bf16[128,2596]{0,1:T(8,128)(2,1)S(1)}, u32[]{:S(2)}, u32[]{:S(2)}) %collective-permute-start.2) | collective-permute-done | bytes 664608 | tf_op jit(solution)/shard_map/ppermute | solution.py:137
  157.6 23.8 %collective-permute-done = bf16[128,2596]{0,1:T(8,128)(2,1)} collective-permute-done((bf16[128,2596]{0,1:T(8,128)(2,1)S(1)}, bf16[128,2596]{0,1:T(8,128)(2,1)}, u32[]{:S(2)}, u32[]{:S(2)}) %collective-permute-start) | collective-permute-done | bytes 664608 | tf_op jit(solution)/shard_map/ppermute | solution.py:137
  181.3 1.4 copy.78
  182.8 0.9 bitcast_dynamic-update-slice_fusion.2
  184.0 0.9 bitcast_dynamic-update-slice_fusion
  184.9 0.9 constant_dynamic-update-slice_fusion.6
  185.8 0.9 bitcast_dynamic-update-slice_fusion.5
  186.7 0.9 bitcast_dynamic-update-slice_fusion.3
  187.6 0.9 bitcast_dynamic-update-slice_fusion.1
  188.6 0.9 constant_dynamic-update-slice_fusion.5
  189.5 2.0 %constant_dynamic-slice_fusion.3 = bf16[4,128,2596]{2,1,0:T(8,128)(2,1)S(1)} fusion(bf16[8,128,2596]{2,1,0:T(8,128)(2,1)} %constant_dynamic-update-slice_fusion.5, s32[]{:T(128)S(6)} %select_n.63), kind=kLoop, calls=%fused_computation.49 | loop fusion | bytes 5316612 | tf_op jit(solution)/shard_map/jit(_roll_dynamic)/dynamic_slice | solution.py:141
  191.4 0.8 slice.68
  192.6 0.7 copy.85
  193.3 1.5 copy.89
  (48 shorter events, 6.0 us)
Async XLA Ops:
  0.6 9.4 %copy-start = (bf16[1,1,512,512]{3,2,1,0:T(8,128)(2,1)S(1)}, bf16[1,1,512,512]{3,2,1,0:T(8,128)(2,1)}, u32[]{:S(2)}) copy-start(bf16[1,1,512,512]{3,2,1,0:T(8,128)(2,1)} %param.17) | copy-start | bytes 1572868
  11.8 80.7 %copy-start.7 = (f32[36,2]{0,1:T(2,128)S(1)}, f32[36,2]{0,1:T(2,128)}, u32[]{:S(2)}) copy-start(f32[36,2]{0,1:T(2,128)} %param.26) | copy-start | bytes 868
  11.8 80.7 %copy-start.8 = (f32[36,2]{0,1:T(2,128)S(1)}, f32[36,2]{0,1:T(2,128)}, u32[]{:S(2)}) copy-start(f32[36,2]{0,1:T(2,128)} %param.27) | copy-start | bytes 868
  11.8 80.8 %copy-start.9 = (f32[36,2]{0,1:T(2,128)S(1)}, f32[36,2]{0,1:T(2,128)}, u32[]{:S(2)}) copy-start(f32[36,2]{0,1:T(2,128)} %param.28) | copy-start | bytes 868
  11.8 110.8 %copy-start.4 = (f32[8,512]{1,0:T(8,128)S(1)}, f32[8,512]{1,0:T(8,128)}, u32[]{:S(2)}) copy-start(f32[8,512]{1,0:T(8,128)} %param.20) | copy-start | bytes 49156
  11.8 110.8 %copy-start.5 = (f32[8,512]{1,0:T(8,128)S(1)}, f32[8,512]{1,0:T(8,128)}, u32[]{:S(2)}) copy-start(f32[8,512]{1,0:T(8,128)} %param.22) | copy-start | bytes 49156
  11.8 110.8 %copy-start.6 = (f32[8,512]{1,0:T(8,128)S(1)}, f32[8,512]{1,0:T(8,128)}, u32[]{:S(2)}) copy-start(f32[8,512]{1,0:T(8,128)} %param.21) | copy-start | bytes 49156
  11.8 111.4 %copy-start.1 = (f32[2,8,1024]{2,1,0:T(8,128)S(1)}, f32[2,8,1024]{2,1,0:T(8,128)}, u32[]{:S(2)}) copy-start(f32[2,8,1024]{2,1,0:T(8,128)} %param.23) | copy-start | bytes 196612
  11.8 111.4 %copy-start.2 = (f32[2,8,1024]{2,1,0:T(8,128)S(1)}, f32[2,8,1024]{2,1,0:T(8,128)}, u32[]{:S(2)}) copy-start(f32[2,8,1024]{2,1,0:T(8,128)} %param.25) | copy-start | bytes 196612
  11.8 111.4 %copy-start.3 = (f32[2,8,1024]{2,1,0:T(8,128)S(1)}, f32[2,8,1024]{2,1,0:T(8,128)}, u32[]{:S(2)}) copy-start(f32[2,8,1024]{2,1,0:T(8,128)} %param.24) | copy-start | bytes 196612
  11.9 77.5 %all-to-all-start = ((bf16[64,8,2596]{2,1,0:T(8,128)(2,1)}), bf16[64,8,2596]{2,1,0:T(8,128)(2,1)S(1)}, u32[]{:S(2)}, u32[]{:S(2)}) async-start(bf16[64,8,2596]{2,1,0:T(8,128)(2,1)} %pad_maximum_fusion), calls=%async_computation | async-start | bytes 5505024 | tf_op jit(solution)/shard_map/all_to_all | solution.py:59
  105.3 15.9 %all-to-all-start.1 = ((f32[64,1,1]{2,1,0:T(1,128)}), f32[64,1,1]{2,1,0:T(1,128)S(1)}, u32[]{:S(2)}, u32[]{:S(2)}) async-start(f32[64,1,1]{2,1,0:T(1,128)} %broadcast_in_dim.28), calls=%async_computation.1 | async-start | bytes 65536 | tf_op jit(solution)/shard_map/all_to_all | solution.py:84
  146.6 10.6 %collective-permute-start.2 = (bf16[128,2596]{0,1:T(8,128)(2,1)S(1)}, bf16[128,2596]{0,1:T(8,128)(2,1)S(1)}, u32[]{:S(2)}, u32[]{:S(2)}) collective-permute-start(bf16[128,2596]{0,1:T(8,128)(2,1)S(1)} %copy.77), channel_id=1, source_target_pairs={{0,64},{64,128},{128,192},{192,0},{1,65},{65,129},{129,193},{193,1... | collective-permute-start | bytes 1993736 | tf_op jit(solution)/shard_map/ppermute | solution.py:137
  148.6 35.1 %collective-permute-start.1 = (bf16[128,2596]{0,1:T(8,128)(2,1)S(1)}, bf16[128,2596]{0,1:T(8,128)(2,1)S(1)}, u32[]{:S(2)}, u32[]{:S(2)}) collective-permute-start(bf16[128,2596]{0,1:T(8,128)(2,1)S(1)} %copy.77), channel_id=1, source_target_pairs={{0,128},{64,192},{128,0},{192,64},{1,129},{65,193},{129,1},{193,65... | collective-permute-start | bytes 1993736 | tf_op jit(solution)/shard_map/ppermute | solution.py:137
  149.2 32.2 %collective-permute-start = (bf16[128,2596]{0,1:T(8,128)(2,1)S(1)}, bf16[128,2596]{0,1:T(8,128)(2,1)}, u32[]{:S(2)}, u32[]{:S(2)}) collective-permute-start(bf16[128,2596]{0,1:T(8,128)(2,1)S(1)} %copy.77), channel_id=1, source_target_pairs={{0,192},{64,0},{128,64},{192,128},{1,193},{65,1},{129,65},{193,129... | collective-permute-start | bytes 1993736 | tf_op jit(solution)/shard_map/ppermute | solution.py:137
